TPU v7x, 256 devices: a whole 4x4x8 slice. The times are simulated.
256 devices in a mesh: dp: 32 (over y, z), tensor: 8 (over x, core).
Axes of the slice: x: 4, y: 4, z: 8, core: 2. Of those that a mesh axis runs over, the one named last changes fastest.
Arguments:
- hidden_in: bfloat16 [1024, 8192], P('dp'), may hold values from -40 to 40
- norm_gain: bfloat16 [8192], P('dp'), may hold values from 0.25 to 2.5
- query_weight: bfloat16 [8192, 8192], P('dp', 'tensor'), may hold values from -0.0625 to 0.0625
- key_weight: bfloat16 [8192, 1024], P('dp', 'tensor'), may hold values from -0.0625 to 0.0625
- value_weight: bfloat16 [8192, 1024], P('dp', 'tensor'), may hold values from -0.0625 to 0.0625
- output_weight: bfloat16 [8192, 8192], P('tensor', 'dp'), may hold values from -0.25 to 0.25
- key_value_cache: bfloat16 [1024, 256, 2, 8, 128], P('dp', None, None, 'tensor'), may hold values from -150 to 150, as said below
- cache_lengths: int32 [1024], replicated, may hold values from 2 to 256, as said below
- parent_beam: int32 [1024], replicated, may hold values from 0 to 1023, as said below
- beam_alive: int32 [1024], replicated, may hold values 0 or 1
Outputs:
- attention_out: bfloat16 [1024, 8192], P(None, 'dp')
Inputs may be any that keep to these rules, and one draw needn't show every extreme that they name: `parent_beam`: among the beams of one device, at most 2 have parents that lie on any one device (beam i lies on device i // 32); on every device some device holds exactly 2 of their parents. `cache_lengths`: some beam holds exactly 256 tokens. `key_value_cache`: slots at or past a beam's length hold arbitrary values.
All inputs are finite; a program needn't handle non-finite values.
Results may differ from a plain program's by a relative error of at most 0.012.
Values may be sent and summed in bfloat16 or wider, within the bound.
No kernel may reach another device: no remote copies, remote signals or barrier semaphores. Data moves between devices by JAX's collectives and lax.ppermute only.
A program may use at most 128 MiB of HBM per device.

v0:
```python
import math
import jax
import jax.numpy as jnp
from jax import lax
from jax.sharding import PartitionSpec as P

HEAD_DIM = 128


def rotate(vectors, position):
    half_width = vectors.shape[-1] // 2
    pair_index = jnp.arange(half_width).astype(jnp.float32)
    frequency = jnp.exp(pair_index * (-2.0 * math.log(1000000.0) / vectors.shape[-1]))
    angles = position.astype(jnp.float32)[:, None] * frequency[None, :]
    cosine = jnp.cos(angles)[:, None, :]
    sine_part = jnp.sin(angles)[:, None, :]
    first_half = vectors[..., :half_width]
    second = vectors[..., half_width:]
    return jnp.concatenate(
        [first_half * cosine - second * sine_part, second * cosine + first_half * sine_part],
        axis=-1,
    )


def attend(queries, key_rows, value_rows, key_new, value_new, length_row):
    row_count, head_total, head_width = queries.shape
    groups = key_rows.shape[2]
    length = key_rows.shape[1]
    grouped = queries.reshape(row_count, groups, head_total // groups, head_width)
    score_scale = 1.0 / math.sqrt(head_width)
    cached = (
        jnp.einsum("rkgd,rlkd->rkgl", grouped, key_rows, preferred_element_type=jnp.float32)
        * score_scale
    )
    latest = (
        jnp.einsum("rkgd,rkd->rkg", grouped, key_new, preferred_element_type=jnp.float32)
        * score_scale
    )
    is_valid = (jnp.arange(length, dtype=jnp.int32)[None, :] < length_row[:, None])[
        :, None, None, :
    ]
    cached = jnp.where(is_valid, cached, -jnp.inf)
    highest = jnp.maximum(jnp.max(cached, axis=-1), latest)
    cached_exp = jnp.exp(cached - highest[..., None])
    latest_exp = jnp.exp(latest - highest)
    denominator = jnp.sum(cached_exp, axis=-1) + latest_exp
    cached_weight = (cached_exp / denominator[..., None]).astype(jnp.bfloat16)
    latest_weight = (latest_exp / denominator).astype(jnp.bfloat16)
    mixture = jnp.einsum(
        "rkgl,rlkd->rkgd", cached_weight, value_rows, preferred_element_type=jnp.float32
    )
    mixture = (
        mixture
        + latest_weight.astype(jnp.float32)[..., None]
        * value_new.astype(jnp.float32)[:, :, None, :]
    )
    return mixture.reshape(row_count, head_total * head_width).astype(jnp.bfloat16)


def arrival_ranks(sources):
    ordinal = jnp.arange(sources.shape[-1], dtype=jnp.int32)
    earlier = (sources[..., None, :] == sources[..., :, None]) & (
        ordinal[None, :] < ordinal[:, None]
    )
    return jnp.sum(earlier.astype(jnp.int32), axis=-1)


def body(
    hidden_in,
    norm_gain,
    query_weight,
    key_weight,
    value_weight,
    output_weight,
    key_value_cache,
    cache_lengths,
    parent_beam,
    beam_alive,
):
    device_count = lax.axis_size("dp")
    device_rank = lax.axis_index("dp")
    local_beams = hidden_in.shape[0]
    capacity = max(2, (2 * local_beams + device_count - 1) // device_count)
    hidden_float = hidden_in.astype(jnp.float32)
    inverse = lax.rsqrt(jnp.mean(hidden_float * hidden_float, axis=1) + 1e-06)
    blocked = lax.all_to_all(hidden_in, "dp", split_axis=1, concat_axis=0, tiled=True)
    scaled = (blocked.astype(jnp.float32) * norm_gain.astype(jnp.float32)[None, :]).astype(
        jnp.bfloat16
    )
    query_width = query_weight.shape[1]
    key_width = key_weight.shape[1]
    summed = (
        lax.psum_scatter(
            jnp.concatenate(
                [
                    jnp.dot(scaled, query_weight, preferred_element_type=jnp.float32),
                    jnp.dot(scaled, key_weight, preferred_element_type=jnp.float32),
                    jnp.dot(scaled, value_weight, preferred_element_type=jnp.float32),
                ],
                axis=1,
            ),
            "dp",
            scatter_dimension=0,
            tiled=True,
        )
        * inverse[:, None]
    )
    first_beam = device_rank * local_beams
    my_parent = lax.dynamic_slice_in_dim(parent_beam, first_beam, local_beams)
    my_alive = lax.dynamic_slice_in_dim(beam_alive, first_beam, local_beams)
    position = jnp.take(cache_lengths, my_parent)
    head_count = query_width // HEAD_DIM
    group_count = key_width // HEAD_DIM
    queries = rotate(
        summed[:, :query_width].reshape(local_beams, head_count, HEAD_DIM), position
    ).astype(jnp.bfloat16)
    key_new = rotate(
        summed[:, query_width : query_width + key_width].reshape(
            local_beams, group_count, HEAD_DIM
        ),
        position,
    ).astype(jnp.bfloat16)
    value_new = (
        summed[:, query_width + key_width :]
        .reshape(local_beams, group_count, HEAD_DIM)
        .astype(jnp.bfloat16)
    )
    source = my_parent // local_beams
    target = source * capacity + arrival_ranks(source)
    slot_total = device_count * capacity
    all_parents = parent_beam.reshape(device_count, local_beams)
    all_sources = all_parents // local_beams
    destination = jnp.broadcast_to(
        jnp.arange(device_count, dtype=jnp.int32)[:, None], (device_count, local_beams)
    )
    placed = jnp.where(
        all_sources == device_rank, destination * capacity + arrival_ranks(all_sources), slot_total
    )
    outgoing = (
        jnp.zeros((slot_total,), jnp.int32)
        .at[placed.reshape(-1)]
        .set((all_parents % local_beams).reshape(-1), mode="drop")
    )
    packed = jnp.take(key_value_cache, outgoing, axis=0)
    arrived = lax.all_to_all(
        packed.reshape((device_count, capacity) + key_value_cache.shape[1:]),
        "dp",
        split_axis=0,
        concat_axis=0,
        tiled=True,
    )
    inherited = jnp.take(arrived.reshape((slot_total,) + key_value_cache.shape[1:]), target, axis=0)
    attention = attend(
        queries, inherited[:, :, 0], inherited[:, :, 1], key_new, value_new, position
    )
    attention = jnp.where(my_alive[:, None] > 0, attention, jnp.zeros_like(attention))
    partial_sum = jnp.dot(
        lax.all_gather(attention, "dp", axis=0, tiled=True),
        output_weight,
        preferred_element_type=jnp.float32,
    )
    return lax.psum(partial_sum, "tensor").astype(jnp.bfloat16)


def solution(mesh):
    placed = (
        P("dp", None),
        P("dp"),
        P("dp", "tensor"),
        P("dp", "tensor"),
        P("dp", "tensor"),
        P("tensor", "dp"),
        P("dp", None, None, "tensor", None),
        P(),
        P(),
        P(),
    )
    return jax.shard_map(body, mesh=mesh, in_specs=placed, out_specs=P(None, "dp"), check_vma=False)
```

profile of v0, /device:TPU:7, one launch (start us, length us, event | category | flops | bytes accessed | tf_op | source)
XLA Modules:
  0.0 547.3 jit_solution(13126944515399061592)
XLA Ops:
  6.5 2.0 copy.55
  8.5 11.2 %all-to-all-start = ((bf16[32,32,256]{2,0,1:T(8,128)(2,1)}), bf16[32,32,256]{2,0,1:T(8,128)(2,1)S(1)}, u32[]{:S(2)}, u32[]{:S(2)}) async-start(bf16[32,32,256]{2,0,1:T(8,128)(2,1)} %bitcast.55), calls=%async_computation | async-start | bytes 1048576 | tf_op jit(solution)/shard_map/all_to_all | solution.py:86
  19.7 0.8 reshape.348
  20.5 0.8 convert_reduce_fusion
  21.3 0.1 broadcast_add_fusion
  21.4 0.1 add.98
  21.5 0.7 add_select_fusion.1
  22.2 4.3 scatter_custom_fusion
  26.5 20.7 %gather_fusion.1 = bf16[64,256,2,128]{3,2,1,0:T(2,128)(2,1)} fusion(bf16[32,256,2,128]{3,2,1,0:T(2,128)(2,1)} %bitcast.57, s32[1024]{0:T(1024)S(1)} %pad_clamp_fusion.1), kind=kCustom, calls=%fused_computation.1 | custom fusion | bytes 16777472 | tf_op jit(solution)/shard_map/jit(_take)/gather | solution.py:144
  47.2 8.9 %copy.41 = bf16[64,256,2,128]{3,1,2,0:T(8,128)(2,1)} copy(bf16[64,256,2,128]{3,2,1,0:T(2,128)(2,1)} %gather_fusion.1) | data formatting | bytes 16777216 | tf_op jit(solution)/shard_map/jit(_take)/gather | solution.py:144
  56.1 0.1 broadcast_in_dim.106
  56.2 7.5 %broadcast_select_fusion = bf16[32,2,256,2,1,128]{5,2,3,1,4,0:T(8,128)(2,1)} fusion(bf16[32,2,256,2,1,128]{5,2,3,1,4,0:T(8,128)(2,1)} %bitcast.56, pred[32,2]{1,0:T(8,128)(4,1)S(1)} %broadcast_in_dim.106), kind=kLoop, calls=%fused_computation.4 | loop fusion | flops 4194304 | bytes 16777280 | tf_op jit(solution)/shard_map/jit(_take)/select_n | solution.py:144
  63.7 9.6 %all-to-all-start.1 = ((bf16[32,2,256,2,1,128]{5,2,3,1,4,0:T(8,128)(2,1)}), bf16[32,2,256,2,1,128]{5,2,3,1,4,0:T(8,128)(2,1)}, u32[]{:S(2)}, u32[]{:S(2)}) async-start(bf16[32,2,256,2,1,128]{5,2,3,1,4,0:T(8,128)(2,1)} %broadcast_select_fusion), calls=%async_computation.1 | async-start | bytes 16777216 | tf_op jit(solution)/shard_map/all_to_all | solution.py:145
  73.3 0.0 reduce-scatter.4.cloned.1.call-start
  73.4 0.1 fusion.6
  73.5 0.3 fusion.38
  73.8 0.3 fusion.37
  74.1 0.8 fusion.36
  74.9 2.8 pad_maximum_fusion
  77.7 5.9 %copy.45 = f32[1024,1280]{1,0:T(8,128)} copy(f32[1024,1280]{0,1:T(8,128)} %pad_maximum_fusion) | data formatting | bytes 10485760
  83.6 0.0 reduce-scatter.4.cloned.1.call-update
  83.6 0.2 all-gather.2.cloned.1.call-start
  83.8 0.8 compare_select_fusion.6
  84.6 0.7 gather_fusion
  85.3 0.8 dynamic-slice_compare_fusion
  86.1 0.2 convert_reduce_fusion.1
  86.3 0.2 multiply_reduce_fusion
  86.5 0.1 iota_compare_fusion
  86.6 0.1 multiply_cosine_fusion.1
  86.8 306.2 %reduce-scatter.4.cloned.1.call-done = f32[32,1280]{1,0:T(8,128)} async-done(((f32[1024,1280]{1,0:T(8,128)}), f32[32,1280]{1,0:T(8,128)}) %reduce-scatter.4.cloned.1.call-update) | async-done | bytes 163856 | tf_op jit(solution)/shard_map/reduce_scatter | solution.py:93
  392.9 1.0 broadcast_multiply_fusion
  394.0 0.1 fusion.25
  394.1 0.1 maximum_bitcast_fusion
  394.2 0.1 subtract_convert_fusion
  394.3 0.2 fusion.19
  394.6 0.0 all-to-all-done.1
  394.6 6.4 %gather_fusion.2 = bf16[32,256,2,128]{3,1,2,0:T(8,128)(2,1)} fusion(bf16[64,256,2,128]{3,1,2,0:T(8,128)(2,1)} %bitcast.4, s32[1024]{0:T(1024)S(1)} %pad_clamp_fusion), kind=kCustom, calls=%fused_computation.2 | custom fusion | bytes 8388736 | tf_op jit(solution)/shard_map/jit(_take)/gather | solution.py:152
  401.0 2.7 bitcast_select_fusion
  403.7 0.0 copy-start.6
  403.7 0.8 fusion.35
  404.4 0.2 fusion.7
  404.7 0.0 copy-start.1
  404.7 0.5 fusion.5
  405.1 0.7 bitcast_select_fusion.1
  405.9 0.0 all-gather.2.cloned.1.call-update
  405.9 76.0 %all-gather.2.cloned.1.call-done = bf16[1024,1024]{1,0:T(8,128)(2,1)} async-done(((bf16[32,1024]{1,0:T(8,128)(2,1)}), bf16[1024,1024]{1,0:T(8,128)(2,1)}) %all-gather.2.cloned.1.call-update) | async-done | bytes 2097168 | tf_op jit(solution)/shard_map/all_gather | solution.py:158
  481.9 2.3 fusion.39
  484.2 56.2 %all-reduce.1 = bf16[1024,256]{1,0:T(8,128)(2,1)} all-reduce(f32[1024,256]{1,0:T(8,128)S(1)} %fusion.39), channel_id=1, replica_groups=mesh['dp'=32,'tensor'=8] {'tensor'}, use_global_device_ids=true, to_apply=%region_7.8 | all-reduce | flops 262144 | bytes 1572864 | tf_op jit(solution)/shard_map/psum | solution.py:162
  (34 shorter events, 0.2 us)
Async XLA Ops:
  6.5 67.6 %copy-start = (bf16[256,1024]{1,0:T(8,128)(2,1)S(1)}, bf16[256,1024]{1,0:T(8,128)(2,1)}, u32[]{:S(2)}) copy-start(bf16[256,1024]{1,0:T(8,128)(2,1)} %param.12) | copy-start | bytes 1572868
  8.5 55.2 %all-to-all-start = ((bf16[32,32,256]{2,0,1:T(8,128)(2,1)}), bf16[32,32,256]{2,0,1:T(8,128)(2,1)S(1)}, u32[]{:S(2)}, u32[]{:S(2)}) async-start(bf16[32,32,256]{2,0,1:T(8,128)(2,1)} %bitcast.55), calls=%async_computation | async-start | bytes 1048576 | tf_op jit(solution)/shard_map/all_to_all | solution.py:86
  63.7 9.7 %copy-start.7 = (bf16[256]{0:T(256)(128)(2,1)S(1)}, bf16[256]{0:T(256)(128)(2,1)}, u32[]{:S(2)}) copy-start(bf16[256]{0:T(256)(128)(2,1)} %param.11) | copy-start | bytes 1540
  63.7 9.8 %copy-start.4 = (bf16[256,128]{1,0:T(8,128)(2,1)S(1)}, bf16[256,128]{1,0:T(8,128)(2,1)}, u32[]{:S(2)}) copy-start(bf16[256,128]{1,0:T(8,128)(2,1)} %param.14) | copy-start | bytes 196612
  63.7 10.1 %copy-start.5 = (bf16[256,128]{1,0:T(8,128)(2,1)S(1)}, bf16[256,128]{1,0:T(8,128)(2,1)}, u32[]{:S(2)}) copy-start(bf16[256,128]{1,0:T(8,128)(2,1)} %param.13) | copy-start | bytes 196612
  63.7 330.9 %all-to-all-start.1 = ((bf16[32,2,256,2,1,128]{5,2,3,1,4,0:T(8,128)(2,1)}), bf16[32,2,256,2,1,128]{5,2,3,1,4,0:T(8,128)(2,1)}, u32[]{:S(2)}, u32[]{:S(2)}) async-start(bf16[32,2,256,2,1,128]{5,2,3,1,4,0:T(8,128)(2,1)} %broadcast_select_fusion), calls=%async_computation.1 | async-start | bytes 16777216 | tf_op jit(solution)/shard_map/all_to_all | solution.py:145
  73.3 319.6 %reduce-scatter.4.cloned.1.call-start = ((), (), s32[]{:S(2)}) async-start(), calls=%async_computation.4 | async-start | bytes 5406720 | tf_op jit(solution)/shard_map/reduce_scatter | solution.py:93
  83.6 1.0 copy-start.2
  83.6 2.7 copy-start.3
  83.6 398.3 %all-gather.2.cloned.1.call-start = ((), (), s32[]{:S(2)}) async-start(), calls=%async_computation.3 | async-start | bytes 2162688 | tf_op jit(solution)/shard_map/all_gather | solution.py:158
  403.7 78.2 %copy-start.6 = (bf16[1024,256]{1,0:T(8,128)(2,1)S(1)}, bf16[1024,256]{1,0:T(8,128)(2,1)}, u32[]{:S(2)}) copy-start(bf16[1024,256]{1,0:T(8,128)(2,1)} %param.15) | copy-start | bytes 1572868
  404.7 135.8 %copy-start.1 = (bf16[256,1024]{1,0:T(8,128)(2,1)S(1)}, bf16[256,1024]{1,0:T(8,128)(2,1)}, u32[]{:S(2)}) copy-start(bf16[256,1024]{1,0:T(8,128)(2,1)} %param.12) | copy-start | bytes 1572868
Sparse Core Ops, SparseCore 0:
  83.7 309.1 reduce-scatter.3
  406.0 75.8 all-gather.1
where the time goes:
time: 548 us; the launch traced here: 547 us
  waiting for transfers between devices  382 us (70%)
  blocking collectives  56.2 us (10%)
  local copies, waits for them, and re-layouts  49.8 us (9%)
  starting transfers between devices  21.1 us (4%)
  other arithmetic  19.1 us (3%)
  between operations  13.7 us (2%)
    reduce_scatter x1, waiting for transfers between devices, body(): lax.psum_scatter(jnp.concatenate([jnp.dot(scaled, query_weight, preferred...  306 us
    all_gather x1, waiting for transfers between devices, body(): lax.all_gather(attention, 'dp', axis=0, tiled=True)  76 us
    psum x1, blocking collectives, body(): return lax.psum(partial_sum, 'tensor').astype(jnp.bfloat16)  56.2 us
    gather x2, local copies, waits for them, and re-layouts, body(): packed = jnp.take(key_value_cache, outgoing, axis=0)  29.6 us
    all_to_all x1, starting transfers between devices, body(): lax.all_to_all(hidden_in, 'dp', split_axis=1, concat_axis=0, tiled=True)  11.2 us
  transfers between devices with their start and end apart: 4, of which 2 were waited for; matrix products, arithmetic and copies ran while one was open for 11% of the time, Pallas kernels for 0%

commit v1 on v0

--- a/solution.py
+++ b/solution.py
@@ -5,6 +5,12 @@
 from jax.sharding import PartitionSpec as P
 
 HEAD_DIM = 128
+
+
+def tiled_gather(x, axis, dim):
+    peers = lax.axis_size(axis)
+    repeats = [peers if d == dim else 1 for d in range(x.ndim)]
+    return lax.all_to_all(jnp.tile(x, repeats), axis, split_axis=dim, concat_axis=dim, tiled=True)
 
 
 def rotate(vectors, position):
@@ -155,9 +161,7 @@
     )
     attention = jnp.where(my_alive[:, None] > 0, attention, jnp.zeros_like(attention))
     partial_sum = jnp.dot(
-        lax.all_gather(attention, "dp", axis=0, tiled=True),
-        output_weight,
-        preferred_element_type=jnp.float32,
+        tiled_gather(attention, "dp", 0), output_weight, preferred_element_type=jnp.float32
     )
     return lax.psum(partial_sum, "tensor").astype(jnp.bfloat16)
 

time: 548 us -> 528 us (0.964)
  waiting for transfers between devices: 382 us -> 311 us
  blocking collectives: 56.2 us -> 109 us
    all_gather x1 -> x0, waiting for transfers between devices: 76 us -> none  [body(): lax.all_gather(attention, 'dp', axis=0, tiled=True)]
    all_to_all x0 -> x1, blocking collectives: none -> 48.3 us  [tiled_gather(): lax.all_to_all(jnp.tile(x, repeats), axis, split_axis=dim, concat_axis=di...]
  transfers between devices with their start and end apart: 4 -> 3, of which waited for: 2 -> 1; matrix products, arithmetic and copies ran while one was open for 11% -> 11% of each run, Pallas kernels for 0% -> 0%
where the time goes in v1:
time: 528 us; the launch traced here: 527 us
  waiting for transfers between devices  311 us (59%)
  blocking collectives  109 us (21%)
  local copies, waits for them, and re-layouts  50.1 us (9%)
  starting transfers between devices  21 us (4%)
  other arithmetic  18.5 us (4%)
  between operations  13.7 us (3%)
    reduce_scatter x1, waiting for transfers between devices, body(): lax.psum_scatter(jnp.concatenate([jnp.dot(scaled, query_weight, preferred...  311 us
    psum x1, blocking collectives, body(): return lax.psum(partial_sum, 'tensor').astype(jnp.bfloat16)  60.8 us
    all_to_all x1, blocking collectives, tiled_gather(): lax.all_to_all(jnp.tile(x, repeats), axis, split_axis=dim, concat_axis=di...  48.3 us
    gather x2, local copies, waits for them, and re-layouts, body(): packed = jnp.take(key_value_cache, outgoing, axis=0)  29.6 us
    all_to_all x1, starting transfers between devices, body(): lax.all_to_all(hidden_in, 'dp', split_axis=1, concat_axis=0, tiled=True)  11.2 us
  transfers between devices with their start and end apart: 3, of which 1 were waited for; matrix products, arithmetic and copies ran while one was open for 11% of the time, Pallas kernels for 0%

profile of v1, /device:TPU:7, one launch (start us, length us, event | category | flops | bytes accessed | tf_op | source)
XLA Modules:
  0.0 526.9 jit_solution(16597566094120505863)
XLA Ops:
  6.5 2.0 copy.55
  8.5 11.2 %all-to-all-start = ((bf16[32,32,256]{2,0,1:T(8,128)(2,1)}), bf16[32,32,256]{2,0,1:T(8,128)(2,1)S(1)}, u32[]{:S(2)}, u32[]{:S(2)}) async-start(bf16[32,32,256]{2,0,1:T(8,128)(2,1)} %bitcast.56), calls=%async_computation | async-start | bytes 1048576 | tf_op jit(solution)/shard_map/all_to_all | solution.py:92
  19.7 0.8 reshape.370
  20.5 0.8 convert_reduce_fusion
  21.3 0.1 broadcast_add_fusion
  21.4 0.1 add.98
  21.5 0.7 add_select_fusion.1
  22.2 4.3 scatter_custom_fusion
  26.5 20.7 %gather_fusion.1 = bf16[64,256,2,128]{3,2,1,0:T(2,128)(2,1)} fusion(bf16[32,256,2,128]{3,2,1,0:T(2,128)(2,1)} %bitcast.58, s32[1024]{0:T(1024)S(1)} %pad_clamp_fusion.1), kind=kCustom, calls=%fused_computation.1 | custom fusion | bytes 16777472 | tf_op jit(solution)/shard_map/jit(_take)/gather | solution.py:150
  47.2 8.9 %copy.41 = bf16[64,256,2,128]{3,1,2,0:T(8,128)(2,1)} copy(bf16[64,256,2,128]{3,2,1,0:T(2,128)(2,1)} %gather_fusion.1) | data formatting | bytes 16777216 | tf_op jit(solution)/shard_map/jit(_take)/gather | solution.py:150
  56.1 0.1 broadcast_in_dim.106
  56.2 7.5 %broadcast_select_fusion = bf16[32,2,256,2,1,128]{5,2,3,1,4,0:T(8,128)(2,1)} fusion(bf16[32,2,256,2,1,128]{5,2,3,1,4,0:T(8,128)(2,1)} %bitcast.57, pred[32,2]{1,0:T(8,128)(4,1)S(1)} %broadcast_in_dim.106), kind=kLoop, calls=%fused_computation.4 | loop fusion | flops 4194304 | bytes 16777280 | tf_op jit(solution)/shard_map/jit(_take)/select_n | solution.py:150
  63.7 0.0 all-to-all-done
  63.7 9.6 %all-to-all-start.1 = ((bf16[32,2,256,2,1,128]{5,2,3,1,4,0:T(8,128)(2,1)}), bf16[32,2,256,2,1,128]{5,2,3,1,4,0:T(8,128)(2,1)}, u32[]{:S(2)}, u32[]{:S(2)}) async-start(bf16[32,2,256,2,1,128]{5,2,3,1,4,0:T(8,128)(2,1)} %broadcast_select_fusion), calls=%async_computation.1 | async-start | bytes 16777216 | tf_op jit(solution)/shard_map/all_to_all | solution.py:151
  73.3 0.2 reduce-scatter.4.cloned.1.call-start
  73.5 0.1 fusion.6
  73.7 0.3 fusion.38
  74.0 0.3 fusion.37
  74.3 0.8 fusion.36
  75.1 2.8 pad_maximum_fusion
  77.9 5.9 %copy.45 = f32[1024,1280]{1,0:T(8,128)} copy(f32[1024,1280]{0,1:T(8,128)} %pad_maximum_fusion) | data formatting | bytes 10485760
  83.8 0.0 reduce-scatter.4.cloned.1.call-update
  83.8 0.8 compare_select_fusion.6
  84.6 0.7 gather_fusion
  85.3 0.8 dynamic-slice_compare_fusion
  86.1 0.2 convert_reduce_fusion.1
  86.3 0.2 multiply_reduce_fusion
  86.6 0.1 iota_compare_fusion
  86.6 0.1 multiply_cosine_fusion.1
  86.8 310.9 %reduce-scatter.4.cloned.1.call-done = f32[32,1280]{1,0:T(8,128)} async-done(((f32[1024,1280]{1,0:T(8,128)}), f32[32,1280]{1,0:T(8,128)}) %reduce-scatter.4.cloned.1.call-update) | async-done | bytes 163856 | tf_op jit(solution)/shard_map/reduce_scatter | solution.py:99
  397.7 1.0 broadcast_multiply_fusion
  398.8 0.1 fusion.25
  398.9 0.1 maximum_bitcast_fusion
  399.0 0.1 subtract_convert_fusion
  399.1 0.2 fusion.19
  399.4 0.0 all-to-all-done.1
  399.4 6.4 %gather_fusion.2 = bf16[32,256,2,128]{3,1,2,0:T(8,128)(2,1)} fusion(bf16[64,256,2,128]{3,1,2,0:T(8,128)(2,1)} %bitcast.4, s32[1024]{0:T(1024)S(1)} %pad_clamp_fusion), kind=kCustom, calls=%fused_computation.2 | custom fusion | bytes 8388736 | tf_op jit(solution)/shard_map/jit(_take)/gather | solution.py:158
  405.8 2.7 bitcast_select_fusion
  408.5 0.8 fusion.35
  409.3 0.2 fusion.7
  409.5 0.0 copy-start.6
  409.5 0.5 fusion.5
  409.9 0.1 bitcast_select_fusion.1
  410.0 0.3 tile.2
  410.3 0.0 copy-start.1
  410.3 48.3 %all_to_all.27 = bf16[32,32,1024]{2,1,0:T(8,128)(2,1)S(1)} all-to-all(bf16[32,32,1024]{2,1,0:T(8,128)(2,1)S(1)} %tile.2), channel_id=1, replica_groups=mesh['dp'=32,'tensor'=8] {'dp'}, dimensions={0} | all-to-all | bytes 4194304 | tf_op jit(solution)/shard_map/all_to_all | solution.py:13
  458.6 0.7 fusion.39
  459.3 60.8 %all-reduce.1 = bf16[1024,256]{1,0:T(8,128)(2,1)} all-reduce(f32[1024,256]{1,0:T(8,128)S(1)} %fusion.39), channel_id=1, replica_groups=mesh['dp'=32,'tensor'=8] {'tensor'}, use_global_device_ids=true, to_apply=%region_7.8 | all-reduce | flops 262144 | bytes 1572864 | tf_op jit(solution)/shard_map/psum | solution.py:166
  (33 shorter events, 0.2 us)
Async XLA Ops:
  6.5 67.8 %copy-start = (bf16[256,1024]{1,0:T(8,128)(2,1)S(1)}, bf16[256,1024]{1,0:T(8,128)(2,1)}, u32[]{:S(2)}) copy-start(bf16[256,1024]{1,0:T(8,128)(2,1)} %param.12) | copy-start | bytes 1572868
  8.5 55.2 %all-to-all-start = ((bf16[32,32,256]{2,0,1:T(8,128)(2,1)}), bf16[32,32,256]{2,0,1:T(8,128)(2,1)S(1)}, u32[]{:S(2)}, u32[]{:S(2)}) async-start(bf16[32,32,256]{2,0,1:T(8,128)(2,1)} %bitcast.56), calls=%async_computation | async-start | bytes 1048576 | tf_op jit(solution)/shard_map/all_to_all | solution.py:92
  63.7 9.8 %copy-start.7 = (bf16[256]{0:T(256)(128)(2,1)S(1)}, bf16[256]{0:T(256)(128)(2,1)}, u32[]{:S(2)}) copy-start(bf16[256]{0:T(256)(128)(2,1)} %param.11) | copy-start | bytes 1540
  63.7 10.0 %copy-start.4 = (bf16[256,128]{1,0:T(8,128)(2,1)S(1)}, bf16[256,128]{1,0:T(8,128)(2,1)}, u32[]{:S(2)}) copy-start(bf16[256,128]{1,0:T(8,128)(2,1)} %param.14) | copy-start | bytes 196612
  63.7 10.3 %copy-start.5 = (bf16[256,128]{1,0:T(8,128)(2,1)S(1)}, bf16[256,128]{1,0:T(8,128)(2,1)}, u32[]{:S(2)}) copy-start(bf16[256,128]{1,0:T(8,128)(2,1)} %param.13) | copy-start | bytes 196612
  63.7 335.7 %all-to-all-start.1 = ((bf16[32,2,256,2,1,128]{5,2,3,1,4,0:T(8,128)(2,1)}), bf16[32,2,256,2,1,128]{5,2,3,1,4,0:T(8,128)(2,1)}, u32[]{:S(2)}, u32[]{:S(2)}) async-start(bf16[32,2,256,2,1,128]{5,2,3,1,4,0:T(8,128)(2,1)} %broadcast_select_fusion), calls=%async_computation.1 | async-start | bytes 16777216 | tf_op jit(solution)/shard_map/all_to_all | solution.py:151
  73.3 324.4 %reduce-scatter.4.cloned.1.call-start = ((), (), s32[]{:S(2)}) async-start(), calls=%async_computation.4 | async-start | bytes 5406720 | tf_op jit(solution)/shard_map/reduce_scatter | solution.py:99
  83.8 0.9 copy-start.2
  83.8 2.5 copy-start.3
  409.5 49.1 %copy-start.6 = (bf16[1024,256]{1,0:T(8,128)(2,1)S(1)}, bf16[1024,256]{1,0:T(8,128)(2,1)}, u32[]{:S(2)}) copy-start(bf16[1024,256]{1,0:T(8,128)(2,1)} %param.15) | copy-start | bytes 1572868
  410.3 109.8 %copy-start.1 = (bf16[256,1024]{1,0:T(8,128)(2,1)S(1)}, bf16[256,1024]{1,0:T(8,128)(2,1)}, u32[]{:S(2)}) copy-start(bf16[256,1024]{1,0:T(8,128)(2,1)} %param.12) | copy-start | bytes 1572868
Sparse Core Ops, SparseCore 0:
  83.9 313.7 reduce-scatter.3
